TPU v7x, 32 devices: a whole 2x2x4 slice. The times are simulated.
32 devices in a mesh: ctx: 8 (over z, x), head: 4 (over y, core).
Axes of the slice: x: 2, y: 2, z: 4, core: 2. Of those that a mesh axis runs over, the one named last changes fastest.
Arguments:
- queries: bfloat16 [4096, 4096], P('ctx', 'head'), may hold values from -6 to 6
- key_states: bfloat16 [4096, 4096], P('ctx', 'head'), may hold values from -6 to 6
- value_states: bfloat16 [4096, 4096], P('ctx', 'head'), may hold values from -6 to 6
- transition_vectors: bfloat16 [4096, 4096], P('ctx', 'head'), may hold values from -6 to 6
- beta_logit: float32 [4096, 32], P('ctx', 'head'), may hold values from -6 to 6
- document_ids: int32 [4096], P('ctx'), may hold values from 0 to 7, as said below
- out_weight: bfloat16 [4096, 4096], P('head'), may hold values from -0.09375 to 0.09375
Outputs:
- layer_out: bfloat16 [4096, 4096], P(('ctx', 'head'))
Inputs may be any that keep to these rules, and one draw needn't show every extreme that they name: `document_ids`: document ids never fall along the sequence; document 0 is the first 2304 tokens; the other documents have 1 or more tokens each and together fill the rest.
All inputs are finite; a program needn't handle non-finite values.
Results may differ from a plain program's by a relative error of at most 0.022.
Values may be sent and summed in bfloat16 or wider, within the bound.
No kernel may reach another device: no remote copies, remote signals or barrier semaphores. Data moves between devices by JAX's collectives and lax.ppermute only.
A program may use at most 128 MiB of HBM per device.

v0:
```python
import jax
import jax.numpy as jnp
from jax import lax
from jax.sharding import PartitionSpec as P

epsilon = 1e-06
masked_value = -1e30
highest = lax.Precision.HIGHEST


def diagonal_blocks(matrix, size):
    count = matrix.shape[0] // size
    tiled = matrix.reshape(count, size, count, size)
    mask = jnp.eye(count, dtype=bool)[:, None, :, None]
    return jnp.sum(jnp.where(mask, tiled, 0.0), axis=2)


def unit_lower_inverse(strict_lower):
    rows_total = strict_lower.shape[0]
    leaf = 16
    leaves = diagonal_blocks(strict_lower, leaf)
    rows = []
    for i in range(leaf):
        row = jnp.broadcast_to(
            (jnp.arange(leaf) == i).astype(jnp.float32), leaves.shape[:1] + (leaf,)
        )
        for m in range(i):
            row = row - leaves[:, i, m][:, None] * rows[m]
        rows.append(row)
    inverse = jnp.stack(rows, axis=1)
    size = leaf
    while size < rows_total:
        pairs = rows_total // (2 * size)
        lower = diagonal_blocks(strict_lower, 2 * size)[:, size:, :size]
        halves = inverse.reshape(pairs, 2, size, size)
        first = halves[:, 0]
        second = halves[:, 1]
        corner = -jnp.einsum(
            "pij,pjk->pik",
            second,
            jnp.einsum("pij,pjk->pik", lower, first, precision=highest),
            precision=highest,
        )
        top = jnp.concatenate([first, jnp.zeros_like(first)], axis=2)
        bottom = jnp.concatenate([corner, second], axis=2)
        inverse = jnp.concatenate([top, bottom], axis=1)
        size *= 2
    return inverse[0]


def lower_solve(strict_lower, right):
    rows_total = strict_lower.shape[0]
    leaf = 16
    count = rows_total // leaf
    if rows_total % leaf or count & count - 1:
        unit_lower = strict_lower + jnp.eye(rows_total, dtype=jnp.float32)
        return lax.linalg.triangular_solve(
            unit_lower, right, left_side=True, lower=True, unit_diagonal=True
        )
    return jnp.dot(unit_lower_inverse(strict_lower), right, precision=highest)


def shard_operators(query_block, key_block, vector_block, strength):
    block_rows = key_block.shape[0]
    head_width = key_block.shape[1]
    row_ids = jnp.arange(block_rows)
    strict = row_ids[:, None] > row_ids[None, :]
    causal = row_ids[:, None] >= row_ids[None, :]
    intersections = jnp.dot(vector_block, vector_block.T, precision=highest)
    strict_lower = jnp.where(strict, intersections * strength[None, :], 0.0)
    key_proj = jnp.where(strict, jnp.dot(vector_block, key_block.T, precision=highest), 0.0)
    solved = lower_solve(strict_lower, jnp.concatenate([key_proj, vector_block], axis=1))
    key_solve = solved[:, :block_rows]
    vector_solve = solved[:, block_rows:]
    weighted = strength[:, None] * vector_block
    keys_end = (key_block - jnp.dot(key_solve.T, weighted, precision=highest)).astype(jnp.bfloat16)
    transfer = jnp.eye(head_width, dtype=jnp.float32) - jnp.dot(
        vector_block.T, strength[:, None] * vector_solve, precision=highest
    )
    query_dots = jnp.where(causal, jnp.dot(query_block, vector_block.T, precision=highest), 0.0)
    scaled_dots = query_dots * strength[None, :]
    intra_scores = jnp.dot(query_block, key_block.T, precision=highest) - jnp.dot(
        scaled_dots, key_solve, precision=highest
    )
    rotated = query_block - jnp.dot(scaled_dots, vector_solve, precision=highest)
    return (intra_scores, keys_end, transfer, rotated)


def on_device(
    queries, key_states, value_states, transition_vectors, beta_logit, document_ids, out_weight
):
    block_rows = queries.shape[0]
    head_count = beta_logit.shape[1]
    head_width = queries.shape[1] // head_count
    score_scale = head_width ** (-0.5)

    def split_heads(flat):
        return jnp.transpose(flat.reshape(block_rows, head_count, head_width), (1, 0, 2))

    query_heads = split_heads(queries).astype(jnp.float32)
    key_heads = split_heads(key_states).astype(jnp.float32)
    value_heads = split_heads(value_states)
    vector_heads = split_heads(transition_vectors).astype(jnp.float32)
    unit_vectors = vector_heads / jnp.sqrt(
        jnp.sum(vector_heads * vector_heads, axis=2, keepdims=True) + epsilon
    )
    strength = 2.0 * jax.nn.sigmoid(beta_logit.T)
    intra_scores, keys_end, transfer, rotated = jax.vmap(shard_operators)(
        query_heads, key_heads, unit_vectors, strength
    )
    row_ids = jnp.arange(block_rows)
    causal = row_ids[:, None] >= row_ids[None, :]
    doc_float = (document_ids + 1).astype(jnp.float32)
    same_doc = doc_float[:, None] == doc_float[None, :]
    own_scores = jnp.where((causal & same_doc)[None], intra_scores * score_scale, masked_value)
    running_max = jnp.max(own_scores, axis=2)
    weights = jnp.exp(own_scores - running_max[..., None])
    running_sum = jnp.sum(weights, axis=2)
    accumulated = jnp.einsum(
        "hqk,hkd->hqd",
        weights.astype(jnp.bfloat16),
        value_heads,
        preferred_element_type=jnp.float32,
    )
    ctx_index = lax.axis_index("ctx")
    ctx_count = lax.axis_size("ctx")
    every_value = lax.all_gather(value_heads, "ctx", axis=1, tiled=True)

    def attend(carried, key_pair, value_pair, transfer_in, key_docs, is_live):
        turned, running_max, running_sum, accumulated = carried
        scores = jnp.einsum(
            "hqd,hkd->hqk",
            turned.astype(jnp.bfloat16),
            key_pair,
            preferred_element_type=jnp.float32,
        )
        allowed = (doc_float[:, None] == key_docs[None, :]) & is_live
        scores = jnp.where(allowed[None], scores * score_scale, masked_value)
        new_max = jnp.maximum(running_max, jnp.max(scores, axis=2))
        factor = jnp.exp(running_max - new_max)
        weights = jnp.exp(scores - new_max[..., None])
        running_sum = running_sum * factor + jnp.sum(weights, axis=2)
        accumulated = accumulated * factor[..., None] + jnp.einsum(
            "hqk,hkd->hqd",
            weights.astype(jnp.bfloat16),
            value_pair,
            preferred_element_type=jnp.float32,
        )
        turned = jnp.einsum("hqd,hde->hqe", turned, transfer_in, precision=highest)
        return (turned, new_max, running_sum, accumulated)

    def visit(carried, key_pair, value_pair, transfer_in, key_docs, is_live):
        return attend(carried, key_pair, value_pair, transfer_in, key_docs, is_live)

    carried = (rotated, running_max, running_sum, accumulated)
    every_key = lax.all_gather(keys_end, "ctx", axis=1, tiled=True)
    every_transfer, every_doc = (
        lax.all_gather(transfer[None].astype(jnp.bfloat16), "ctx", axis=0, tiled=True).astype(
            jnp.float32
        ),
        lax.all_gather(doc_float.astype(jnp.bfloat16), "ctx", axis=0, tiled=True).astype(
            doc_float.dtype
        ),
    )

    def local_step(offset, inner):
        source = jnp.maximum(ctx_index - offset, 0)
        key_pair = lax.dynamic_slice_in_dim(every_key, source * block_rows, block_rows, 1)
        value_pair = lax.dynamic_slice_in_dim(every_value, source * block_rows, block_rows, 1)
        transfer_in = lax.dynamic_index_in_dim(every_transfer, source, 0, keepdims=False)
        key_docs = lax.dynamic_slice_in_dim(every_doc, source * block_rows, block_rows, 0)
        return visit(inner, key_pair, value_pair, transfer_in, key_docs, ctx_index - offset >= 0)

    carried = lax.fori_loop(1, ctx_count, local_step, carried)
    attended = (carried[3] / carried[2][..., None]).astype(jnp.bfloat16)
    token_rows = jnp.transpose(attended, (1, 0, 2)).reshape(block_rows, head_count * head_width)
    return lax.psum_scatter(
        jnp.dot(token_rows, out_weight, preferred_element_type=jnp.float32).astype(jnp.bfloat16),
        "head",
        scatter_dimension=0,
        tiled=True,
    )


def solution(mesh):
    return jax.shard_map(
        on_device,
        mesh=mesh,
        in_specs=(
            P("ctx", "head"),
            P("ctx", "head"),
            P("ctx", "head"),
            P("ctx", "head"),
            P("ctx", "head"),
            P("ctx"),
            P("head", None),
        ),
        out_specs=P(("ctx", "head"), None),
        check_vma=False,
    )
```

profile of v0, /device:TPU:0, one launch (start us, length us, event | category | flops | bytes accessed | tf_op | source)
XLA Modules:
  0.0 1076.8 jit_solution(17737255387501927683)
XLA Ops:
  12.2 9.7 multiply_select_fusion.1
  21.9 9.1 copy.491
  31.0 38.0 %reshape.2370 = f32[8,32,16,32,16]{4,3,2,1,0:T(8,128)} reshape(f32[8,512,512]{2,1,0:T(8,128)} %copy.491) | data formatting | bytes 16777216 | tf_op jit(solution)/shard_map/vmap()/reshape | solution.py:13
  69.0 21.5 %select_reduce_fusion = f32[8,32,16,16]{3,2,1,0:T(8,128)S(1)} fusion(f32[8,32,16,32,16]{4,3,2,1,0:T(8,128)} %reshape.2370, pred[32,32]{1,0:T(8,128)(4,1)S(1)} %iota_compare_fusion.9), kind=kLoop, calls=%fused_computation.26 | loop fusion | flops 4128768 | bytes 8651776 | tf_op jit(solution)/shard_map/vmap()/reduce_sum | solution.py:15
  92.5 5.4 fusion.119
  99.1 5.9 fusion.118
  105.5 6.1 fusion.117
  112.1 5.9 fusion.116
  118.6 6.2 fusion.115
  124.7 6.0 fusion.114
  131.3 20.9 %reshape.2371 = f32[8,16,32,16,32]{2,1,4,3,0:T(8,128)} reshape(f32[8,512,512]{1,2,0:T(8,128)} %multiply_select_fusion.1) | data formatting | bytes 16777216 | tf_op jit(solution)/shard_map/vmap()/reshape | solution.py:13
  152.8 12.9 %reshape.2373 = f32[8,8,64,8,64]{2,1,4,3,0:T(8,128)} reshape(f32[8,512,512]{1,2,0:T(8,128)} %multiply_select_fusion.1) | data formatting | bytes 16777216 | tf_op jit(solution)/shard_map/vmap()/reshape | solution.py:13
  166.2 9.9 reshape.2375
  176.6 10.9 %reshape.2377 = f32[8,2,256,2,256]{2,1,4,3,0:T(2,128)} reshape(f32[8,512,512]{1,2,0:T(8,128)} %multiply_select_fusion.1) | data formatting | bytes 16777216 | tf_op jit(solution)/shard_map/vmap()/reshape | solution.py:13
  475.8 3.5 fusion.97
  479.5 3.5 fusion.96
  483.1 4.2 constant_dynamic-update-slice_fusion.1
  487.5 4.0 constant_dynamic-update-slice_fusion
  491.6 4.8 subtract_dynamic-update-slice_fusion
  497.1 13.7 %select_reduce_fusion.1 = f32[8,16,32,32]{2,1,3,0:T(8,128)S(1)} fusion(f32[8,16,32,16,32]{2,1,4,3,0:T(8,128)} %reshape.2371, pred[16,16]{0,1:T(8,128)(4,1)S(1)} %copy-done.75), kind=kLoop, calls=%fused_computation.27 | loop fusion | flops 4063232 | bytes 8913152 | tf_op jit(solution)/shard_map/vmap()/reduce_sum | solution.py:15
  517.6 9.5 select_reduce_fusion.2
  532.7 6.7 select_reduce_fusion.4
  543.7 12.9 %select_reduce_fusion.3 = f32[8,2,256,256]{2,1,3,0:T(2,128)} fusion(f32[8,2,256,2,256]{2,1,4,3,0:T(2,128)} %reshape.2377, pred[2,2]{0,1:T(4,128)(4,1)S(1)} %copy-done.78), kind=kLoop, calls=%fused_computation.44 | loop fusion | flops 3145728 | bytes 12582916 | tf_op jit(solution)/shard_map/vmap()/reduce_sum | solution.py:15
  565.5 5.1 fusion.54
  577.2 6.1 broadcast_select_fusion
  583.3 26.1 %fusion.22 = f32[8,512,640]{2,1,0:T(8,128)} fusion(f32[8,512,128]{1,2,0:T(8,128)S(1)} %copy-done.1, f32[8,512,512]{1,2,0:T(8,128)} %broadcast_select_fusion, f32[8,1,256,256]{3,2,0,1:T(8,128)} %get-tuple-element.265, f32[8,1,256,256]{3,2,0,1:T(8,128)} %get-tuple-element.264, f32[8,1,256,256]{3,2,0,1:T(8,128)} %negate_bitcast_fusion), kind=kOutput, calls=%fused_computation.29 | convolution fusion | flops 16117137408 | bytes 27262976 | tf_op jit(solution)/shard_map/vmap()/dot_general | solution.py:60
  612.4 3.4 copy.808
  615.9 4.4 fusion.74
  620.4 16.5 %subtract_convert_fusion = bf16[8,512,128]{2,1,0:T(8,128)(2,1)} fusion(f32[8,512,128]{1,2,0:T(8,128)S(1)} %copy-done.1, f32[8,512,640]{2,1,0:T(8,128)} %fusion.22, bf16[512,8,128]{2,0,1:T(8,128)(2,1)S(1)} %copy.753, f32[8,512]{1,0:T(8,128)S(1)} %copy-done.10), kind=kOutput, calls=%fused_computation.81 | convolution fusion | flops 3223322624 | bytes 12599296 | tf_op jit(solution)/shard_map/vmap()/dot_general | solution.py:76
  644.1 4.9 fusion.88
  652.3 16.7 %convert_subtract_fusion = f32[8,512,128]{2,1,0:T(8,128)} fusion(f32[8,512,512]{2,1,0:T(8,128)S(1)} %fusion.88, f32[8,512]{1,0:T(8,128)S(1)} %copy-done.10, pred[512,512]{0,1:T(8,128)(4,1)S(1)} %iota_compare_fusion.7, bf16[512,8,128]{2,0,1:T(8,128)(2,1)S(1)} %copy-done.3, f32[8,512,640]{2,1,0:T(8,128)} %fusion.22), kind=kOutput, calls=%fused_computation.87 | convolution fusion | flops 3226468352 | bytes 13910016 | tf_op jit(solution)/shard_map/vmap()/dot_general | solution.py:85
  671.0 28.1 %all-gather.1 = bf16[8,1,512]{2,1,0:T(2,128)(2,1)S(1)} all-gather(bf16[1,1,512]{2,1,0:T(2,128)(2,1)S(1)} %reshape.2388), channel_id=1, replica_groups=mesh['ctx'=8,'head'=4] {'ctx'}, dimensions={0}, use_global_device_ids=true | all-gather | bytes 9216 | tf_op jit(solution)/shard_map/all_gather | solution.py:161
  699.4 19.2 %fusion.35 = f32[8,512,512]{1,2,0:T(8,128)S(1)} fusion(f32[8,512,640]{2,1,0:T(8,128)} %fusion.22, f32[8,512,512]{2,1,0:T(8,128)} %copy-done.2, f32[8,512]{1,0:T(8,128)S(1)} %copy-done.10, pred[512,512]{0,1:T(8,128)(4,1)S(1)} %iota_compare_fusion.7), kind=kOutput, calls=%fused_computation.49 | convolution fusion | flops 12889096192 | bytes 25444352 | tf_op jit(solution)/shard_map/vmap()/dot_general | solution.py:82
  724.8 4.5 convert.2
  729.3 69.1 %all-gather.6.cloned.1.call-done = bf16[8,4096,128]{2,1,0:T(8,128)(2,1)} async-done(((bf16[8,512,128]{2,1,0:T(8,128)(2,1)}), bf16[8,4096,128]{2,1,0:T(8,128)(2,1)}) %all-gather.6.cloned.1.call-update) | async-done | bytes 8388624 | tf_op jit(solution)/shard_map/all_gather | solution.py:156
  798.4 125.7 %all-gather.8.cloned.1.call-done = bf16[8,4096,128]{1,2,0:T(8,128)(2,1)} async-done(((bf16[8,512,128]{1,2,0:T(8,128)(2,1)}), bf16[8,4096,128]{1,2,0:T(8,128)(2,1)}) %all-gather.8.cloned.1.call-update) | async-done | bytes 8388624 | tf_op jit(solution)/shard_map/all_gather | solution.py:127
  924.0 91.1 %while.19 = (s32[]{:T(128)}, f32[8,512,128]{1,2,0:T(8,128)S(1)}, f32[8,512]{1,0:T(8,128)S(1)}, f32[8,512]{1,0:T(8,128)S(1)}, f32[8,512,128]{2,1,0:T(8,128)}, /*i...) while((s32[]{:T(128)}, f32[8,512,128]{1,2,0:T(8,128)S(1)}, ...), condition=%wide.region_11.12_spmd, body=%wide.region_8.11_spmd.sunk | while | flops 1904222208 | bytes 60563748 | solution.py:174
  929.4 4.3 multiply_add_fusion.5
  933.8 3.4 convolution_bitcast_fusion.2
  942.4 4.3 multiply_add_fusion.5
  955.4 4.3 multiply_add_fusion.5
  968.4 4.3 multiply_add_fusion.5
  981.4 4.3 multiply_add_fusion.5
  994.3 4.3 multiply_add_fusion.5
  1007.3 4.3 multiply_add_fusion.5
  1011.7 3.4 convolution_bitcast_fusion.2
  1017.4 9.5 convolution_convert_fusion
  1026.9 42.9 %reduce-scatter.2.cloned.1.call-done = bf16[128,4096]{1,0:T(8,128)(2,1)} async-done(((bf16[512,4096]{1,0:T(8,128)(2,1)}), bf16[128,4096]{1,0:T(8,128)(2,1)}) %reduce-scatter.2.cloned.1.call-update) | async-done | bytes 1048592 | tf_op jit(solution)/shard_map/reduce_scatter | solution.py:177
  (568 shorter events, 410.0 us)
Async XLA Ops:
  6.5 718.2 %all-gather.10.cloned.1.call-start = ((), (), s32[]{:S(2)}) async-start(), calls=%async_computation.4 | async-start | bytes 2359296 | tf_op jit(solution)/shard_map/all_gather | solution.py:158
  7.2 181.8 %copy-start.41 = (f32[16]{0:T(128)}, f32[16]{0:T(128)S(1)}, u32[]{:S(2)}) copy-start(f32[16]{0:T(128)S(1)} %get-tuple-element.399) | copy-start | bytes 196
  176.6 12.1 %copy-start.11 = (f32[8,32,1,1]{3,2,1,0:T(1,128)S(1)}, f32[8,32,1,1]{3,2,1,0:T(1,128)}, u32[]{:S(2)}) copy-start(f32[8,32,1,1]{3,2,1,0:T(1,128)} %get-tuple-element.393) | copy-start | bytes 3076
  454.5 18.3 %copy-start.12 = (f32[8,16,2]{1,2,0:T(2,128)S(1)}, f32[8,16,2]{1,2,0:T(2,128)}, u32[]{:S(2)}) copy-start(f32[8,16,2]{1,2,0:T(2,128)} %copy.593) | copy-start | bytes 3076
  454.5 18.3 %copy-start.13 = (f32[8,16,2]{1,2,0:T(2,128)S(1)}, f32[8,16,2]{1,2,0:T(2,128)}, u32[]{:S(2)}) copy-start(f32[8,16,2]{1,2,0:T(2,128)} %copy.595) | copy-start | bytes 3076
  454.5 18.3 %copy-start.14 = (f32[8,16,2]{1,2,0:T(2,128)S(1)}, f32[8,16,2]{1,2,0:T(2,128)}, u32[]{:S(2)}) copy-start(f32[8,16,2]{1,2,0:T(2,128)} %copy.597) | copy-start | bytes 3076
  454.5 18.3 %copy-start.15 = (f32[8,16,2]{1,2,0:T(2,128)S(1)}, f32[8,16,2]{1,2,0:T(2,128)}, u32[]{:S(2)}) copy-start(f32[8,16,2]{1,2,0:T(2,128)} %copy.599) | copy-start | bytes 3076
  454.5 18.3 %copy-start.16 = (f32[8,16,2]{1,2,0:T(2,128)S(1)}, f32[8,16,2]{1,2,0:T(2,128)}, u32[]{:S(2)}) copy-start(f32[8,16,2]{1,2,0:T(2,128)} %copy.601) | copy-start | bytes 3076
  454.5 21.1 %copy-start.17 = (f32[8,16,2]{1,2,0:T(2,128)S(1)}, f32[8,16,2]{1,2,0:T(2,128)}, u32[]{:S(2)}) copy-start(f32[8,16,2]{1,2,0:T(2,128)} %copy.603) | copy-start | bytes 3076
  454.5 21.1 %copy-start.18 = (f32[8,16,2]{1,2,0:T(2,128)S(1)}, f32[8,16,2]{1,2,0:T(2,128)}, u32[]{:S(2)}) copy-start(f32[8,16,2]{1,2,0:T(2,128)} %copy.605) | copy-start | bytes 3076
  454.6 21.1 %copy-start.19 = (f32[8,16,2]{1,2,0:T(2,128)S(1)}, f32[8,16,2]{1,2,0:T(2,128)}, u32[]{:S(2)}) copy-start(f32[8,16,2]{1,2,0:T(2,128)} %copy.607) | copy-start | bytes 3076
  454.6 21.1 %copy-start.20 = (f32[8,16,2]{1,2,0:T(2,128)S(1)}, f32[8,16,2]{1,2,0:T(2,128)}, u32[]{:S(2)}) copy-start(f32[8,16,2]{1,2,0:T(2,128)} %copy.609) | copy-start | bytes 3076
  454.6 21.1 %copy-start.21 = (f32[8,16,2]{1,2,0:T(2,128)S(1)}, f32[8,16,2]{1,2,0:T(2,128)}, u32[]{:S(2)}) copy-start(f32[8,16,2]{1,2,0:T(2,128)} %copy.611) | copy-start | bytes 3076
  454.6 21.1 %copy-start.22 = (f32[8,16,2]{1,2,0:T(2,128)S(1)}, f32[8,16,2]{1,2,0:T(2,128)}, u32[]{:S(2)}) copy-start(f32[8,16,2]{1,2,0:T(2,128)} %copy.613) | copy-start | bytes 3076
  454.6 21.1 %copy-start.23 = (f32[8,16,2]{1,2,0:T(2,128)S(1)}, f32[8,16,2]{1,2,0:T(2,128)}, u32[]{:S(2)}) copy-start(f32[8,16,2]{1,2,0:T(2,128)} %copy.615) | copy-start | bytes 3076
  454.6 21.1 %copy-start.24 = (f32[8,16,2]{1,2,0:T(2,128)S(1)}, f32[8,16,2]{1,2,0:T(2,128)}, u32[]{:S(2)}) copy-start(f32[8,16,2]{1,2,0:T(2,128)} %copy.617) | copy-start | bytes 3076
  454.6 21.1 %copy-start.25 = (f32[8,16,2]{1,2,0:T(2,128)S(1)}, f32[8,16,2]{1,2,0:T(2,128)}, u32[]{:S(2)}) copy-start(f32[8,16,2]{1,2,0:T(2,128)} %copy.619) | copy-start | bytes 3076
  454.6 21.1 %copy-start.26 = (f32[8,16,2]{1,2,0:T(2,128)S(1)}, f32[8,16,2]{1,2,0:T(2,128)}, u32[]{:S(2)}) copy-start(f32[8,16,2]{1,2,0:T(2,128)} %copy.621) | copy-start | bytes 3076
  454.6 21.1 %copy-start.27 = (f32[8,16,2]{1,2,0:T(2,128)S(1)}, f32[8,16,2]{1,2,0:T(2,128)}, u32[]{:S(2)}) copy-start(f32[8,16,2]{1,2,0:T(2,128)} %copy.623) | copy-start | bytes 3076
  459.1 20.2 %copy-start.29 = (f32[8,16,2]{1,2,0:T(2,128)S(1)}, f32[8,16,2]{1,2,0:T(2,128)}, u32[]{:S(2)}) copy-start(f32[8,16,2]{1,2,0:T(2,128)} %copy.625) | copy-start | bytes 3076
  459.1 20.2 %copy-start.30 = (f32[8,16,2]{1,2,0:T(2,128)S(1)}, f32[8,16,2]{1,2,0:T(2,128)}, u32[]{:S(2)}) copy-start(f32[8,16,2]{1,2,0:T(2,128)} %copy.627) | copy-start | bytes 3076
  459.1 20.2 %copy-start.31 = (f32[8,16,2]{1,2,0:T(2,128)S(1)}, f32[8,16,2]{1,2,0:T(2,128)}, u32[]{:S(2)}) copy-start(f32[8,16,2]{1,2,0:T(2,128)} %copy.629) | copy-start | bytes 3076
  459.1 20.2 %copy-start.32 = (f32[8,16,2]{1,2,0:T(2,128)S(1)}, f32[8,16,2]{1,2,0:T(2,128)}, u32[]{:S(2)}) copy-start(f32[8,16,2]{1,2,0:T(2,128)} %copy.631) | copy-start | bytes 3076
  459.1 20.2 %copy-start.33 = (f32[8,16,2]{1,2,0:T(2,128)S(1)}, f32[8,16,2]{1,2,0:T(2,128)}, u32[]{:S(2)}) copy-start(f32[8,16,2]{1,2,0:T(2,128)} %copy.633) | copy-start | bytes 3076
  459.1 20.2 %copy-start.34 = (f32[8,16,2]{1,2,0:T(2,128)S(1)}, f32[8,16,2]{1,2,0:T(2,128)}, u32[]{:S(2)}) copy-start(f32[8,16,2]{1,2,0:T(2,128)} %copy.635) | copy-start | bytes 3076
  459.1 20.2 %copy-start.35 = (f32[8,16,2]{1,2,0:T(2,128)S(1)}, f32[8,16,2]{1,2,0:T(2,128)}, u32[]{:S(2)}) copy-start(f32[8,16,2]{1,2,0:T(2,128)} %copy.637) | copy-start | bytes 3076
  459.2 20.2 %copy-start.36 = (f32[8,16,2]{1,2,0:T(2,128)S(1)}, f32[8,16,2]{1,2,0:T(2,128)}, u32[]{:S(2)}) copy-start(f32[8,16,2]{1,2,0:T(2,128)} %copy.639) | copy-start | bytes 3076
  459.2 20.2 %copy-start.37 = (f32[8,16,2]{1,2,0:T(2,128)S(1)}, f32[8,16,2]{1,2,0:T(2,128)}, u32[]{:S(2)}) copy-start(f32[8,16,2]{1,2,0:T(2,128)} %copy.641) | copy-start | bytes 3076
  459.2 20.2 %copy-start.38 = (f32[8,16,2]{1,2,0:T(2,128)S(1)}, f32[8,16,2]{1,2,0:T(2,128)}, u32[]{:S(2)}) copy-start(f32[8,16,2]{1,2,0:T(2,128)} %copy.643) | copy-start | bytes 3076
  459.2 20.2 %copy-start.39 = (f32[8,16,2]{1,2,0:T(2,128)S(1)}, f32[8,16,2]{1,2,0:T(2,128)}, u32[]{:S(2)}) copy-start(f32[8,16,2]{1,2,0:T(2,128)} %copy.645) | copy-start | bytes 3076
  459.2 20.2 %copy-start.40 = (f32[8,16,2]{1,2,0:T(2,128)S(1)}, f32[8,16,2]{1,2,0:T(2,128)}, u32[]{:S(2)}) copy-start(f32[8,16,2]{1,2,0:T(2,128)} %copy.647) | copy-start | bytes 3076
  466.4 20.9 %copy-start.46 = (f32[8,16,2]{1,2,0:T(2,128)S(1)}, f32[8,16,2]{1,2,0:T(2,128)}, u32[]{:S(2)}) copy-start(f32[8,16,2]{1,2,0:T(2,128)} %copy.675) | copy-start | bytes 3076
  466.4 20.9 %copy-start.47 = (f32[8,16,2]{1,2,0:T(2,128)S(1)}, f32[8,16,2]{1,2,0:T(2,128)}, u32[]{:S(2)}) copy-start(f32[8,16,2]{1,2,0:T(2,128)} %copy.677) | copy-start | bytes 3076
  466.5 20.9 %copy-start.48 = (f32[8,16,2]{1,2,0:T(2,128)S(1)}, f32[8,16,2]{1,2,0:T(2,128)}, u32[]{:S(2)}) copy-start(f32[8,16,2]{1,2,0:T(2,128)} %copy.679) | copy-start | bytes 3076
  466.5 20.9 %copy-start.49 = (f32[8,16,2]{1,2,0:T(2,128)S(1)}, f32[8,16,2]{1,2,0:T(2,128)}, u32[]{:S(2)}) copy-start(f32[8,16,2]{1,2,0:T(2,128)} %copy.681) | copy-start | bytes 3076
  466.5 20.9 %copy-start.50 = (f32[8,16,2]{1,2,0:T(2,128)S(1)}, f32[8,16,2]{1,2,0:T(2,128)}, u32[]{:S(2)}) copy-start(f32[8,16,2]{1,2,0:T(2,128)} %copy.683) | copy-start | bytes 3076
  466.5 20.9 %copy-start.51 = (f32[8,16,2]{1,2,0:T(2,128)S(1)}, f32[8,16,2]{1,2,0:T(2,128)}, u32[]{:S(2)}) copy-start(f32[8,16,2]{1,2,0:T(2,128)} %copy.685) | copy-start | bytes 3076
  466.5 20.9 %copy-start.52 = (f32[8,16,2]{1,2,0:T(2,128)S(1)}, f32[8,16,2]{1,2,0:T(2,128)}, u32[]{:S(2)}) copy-start(f32[8,16,2]{1,2,0:T(2,128)} %copy.687) | copy-start | bytes 3076
  466.5 20.9 %copy-start.53 = (f32[8,16,2]{1,2,0:T(2,128)S(1)}, f32[8,16,2]{1,2,0:T(2,128)}, u32[]{:S(2)}) copy-start(f32[8,16,2]{1,2,0:T(2,128)} %copy.689) | copy-start | bytes 3076
  470.4 17.0 %copy-start.54 = (f32[8,16,2]{1,2,0:T(2,128)S(1)}, f32[8,16,2]{1,2,0:T(2,128)}, u32[]{:S(2)}) copy-start(f32[8,16,2]{1,2,0:T(2,128)} %copy.691) | copy-start | bytes 3076
  470.4 17.0 %copy-start.55 = (f32[8,16,2]{1,2,0:T(2,128)S(1)}, f32[8,16,2]{1,2,0:T(2,128)}, u32[]{:S(2)}) copy-start(f32[8,16,2]{1,2,0:T(2,128)} %copy.693) | copy-start | bytes 3076
  470.4 17.0 %copy-start.56 = (f32[8,16,2]{1,2,0:T(2,128)S(1)}, f32[8,16,2]{1,2,0:T(2,128)}, u32[]{:S(2)}) copy-start(f32[8,16,2]{1,2,0:T(2,128)} %copy.695) | copy-start | bytes 3076
  470.4 17.0 %copy-start.57 = (f32[8,16,2]{1,2,0:T(2,128)S(1)}, f32[8,16,2]{1,2,0:T(2,128)}, u32[]{:S(2)}) copy-start(f32[8,16,2]{1,2,0:T(2,128)} %copy.697) | copy-start | bytes 3076
  479.4 12.1 %copy-start.63 = (f32[16]{0:T(128)S(1)}, f32[16]{0:T(128)}, u32[]{:S(2)}) copy-start(f32[16]{0:T(128)} %get-tuple-element.404) | copy-start | bytes 196
  620.3 178.0 %all-gather.6.cloned.1.call-start = ((), (), s32[]{:S(2)}) async-start(), calls=%async_computation.1 | async-start | bytes 9437184 | tf_op jit(solution)/shard_map/all_gather | solution.py:156
  636.9 287.1 %all-gather.8.cloned.1.call-start = ((), (), s32[]{:S(2)}) async-start(), calls=%async_computation.2 | async-start | bytes 9437184 | tf_op jit(solution)/shard_map/all_gather | solution.py:127
  639.3 430.5 %reduce-scatter.2.cloned.1.call-start = ((), (), s32[]{:S(2)}) async-start(), calls=%async_computation.3 | async-start | bytes 5242880 | tf_op jit(solution)/shard_map/reduce_scatter | solution.py:177
  699.3 19.2 %copy-start.4 = (bf16[512,8,128]{2,0,1:T(8,128)(2,1)S(1)}, bf16[512,8,128]{2,0,1:T(8,128)(2,1)}, u32[]{:S(2)}) copy-start(bf16[512,8,128]{2,0,1:T(8,128)(2,1)} %copy.485) | copy-start | bytes 3145732
  (48 other events, 297.3 us)
Sparse Core Ops, SparseCore 0:
  620.5 51.9 all-gather.9
  674.7 123.6 all-gather.5
  800.4 123.5 all-gather.7
  1027.0 42.7 reduce-scatter.1
where the time goes:
time: 1100 us; the launch traced here: 1080 us
  local copies, waits for them, and re-layouts  449 us (41%)
  waiting for transfers between devices  238 us (22%)
  matrix products  215 us (20%)
  other arithmetic  130 us (12%)
  blocking collectives  28.1 us (3%)
  between operations  15.2 us (1%)
    slice x127, local copies, waits for them, and re-layouts, unit_lower_inverse(): row = row - leaves[:, i, m][:, None] * rows[m]  211 us
    all_gather x1, waiting for transfers between devices, on_device(): every_value = lax.all_gather(value_heads, 'ctx', axis=1, tiled=True)  126 us
    mul x120, local copies, waits for them, and re-layouts, unit_lower_inverse(): row = row - leaves[:, i, m][:, None] * rows[m]  97 us
    reshape x5, local copies, waits for them, and re-layouts, diagonal_blocks(): tiled = matrix.reshape(count, size, count, size)  92.6 us
    all_gather x1, waiting for transfers between devices, on_device(): every_key = lax.all_gather(keys_end, 'ctx', axis=1, tiled=True)  69.1 us
    reduce_sum x5, other arithmetic, diagonal_blocks(): return jnp.sum(jnp.where(mask, tiled, 0.0), axis=2)  64.2 us
    reduce_scatter x1, waiting for transfers between devices, on_device(): lax.psum_scatter(jnp.dot(token_rows, out_weight, preferred_element_type=j...  42.9 us
    unnamed x14, other arithmetic  30.7 us
  transfers between devices with their start and end apart: 4, of which 3 were waited for; matrix products, arithmetic and copies ran while one was open for 7% of the time, Pallas kernels for 0%

commit v1 on v0

--- a/solution.py
+++ b/solution.py
@@ -124,7 +124,6 @@
     )
     ctx_index = lax.axis_index("ctx")
     ctx_count = lax.axis_size("ctx")
-    every_value = lax.all_gather(value_heads, "ctx", axis=1, tiled=True)
 
     def attend(carried, key_pair, value_pair, transfer_in, key_docs, is_live):
         turned, running_max, running_sum, accumulated = carried
@@ -153,7 +152,11 @@
         return attend(carried, key_pair, value_pair, transfer_in, key_docs, is_live)
 
     carried = (rotated, running_max, running_sum, accumulated)
-    every_key = lax.all_gather(keys_end, "ctx", axis=1, tiled=True)
+    every_value, every_key = jnp.split(
+        lax.all_gather(jnp.concatenate([value_heads, keys_end], axis=0), "ctx", axis=1, tiled=True),
+        [value_heads.shape[0]],
+        axis=0,
+    )
     every_transfer, every_doc = (
         lax.all_gather(transfer[None].astype(jnp.bfloat16), "ctx", axis=0, tiled=True).astype(
             jnp.float32

time: 1100 us -> 1080 us (0.982)
  waiting for transfers between devices: 238 us -> 212 us
  local copies, waits for them, and re-layouts: 449 us -> 463 us
    all_gather x2 -> x1, waiting for transfers between devices: 195 us -> 169 us  [on_device(): lax.all_gather(jnp.concatenate([value_heads, keys_end], axis=0), 'ctx', a...]
    split x0 -> x1, local copies, waits for them, and re-layouts: none -> 11.4 us  [on_device(): jnp.split(lax.all_gather(jnp.concatenate([value_heads, keys_end], axis=0)...]
  transfers between devices with their start and end apart: 4 -> 3, of which waited for: 3 -> 2; matrix products, arithmetic and copies ran while one was open for 7% -> 7% of each run, Pallas kernels for 0% -> 0%
where the time goes in v1:
time: 1080 us; the launch traced here: 1070 us
  local copies, waits for them, and re-layouts  463 us (43%)
  matrix products  214 us (20%)
  waiting for transfers between devices  212 us (20%)
  other arithmetic  131 us (12%)
  blocking collectives  28.3 us (3%)
  between operations  15.2 us (1%)
    slice x127, local copies, waits for them, and re-layouts, unit_lower_inverse(): row = row - leaves[:, i, m][:, None] * rows[m]  212 us
    all_gather x1, waiting for transfers between devices, on_device(): lax.all_gather(jnp.concatenate([value_heads, keys_end], axis=0), 'ctx', a...  169 us
    mul x120, local copies, waits for them, and re-layouts, unit_lower_inverse(): row = row - leaves[:, i, m][:, None] * rows[m]  97 us
    reshape x5, local copies, waits for them, and re-layouts, diagonal_blocks(): tiled = matrix.reshape(count, size, count, size)  92.6 us
    reduce_sum x5, other arithmetic, diagonal_blocks(): return jnp.sum(jnp.where(mask, tiled, 0.0), axis=2)  64.2 us
    reduce_scatter x1, waiting for transfers between devices, on_device(): lax.psum_scatter(jnp.dot(token_rows, out_weight, preferred_element_type=j...  42.8 us
    unnamed x14, other arithmetic  30.7 us
    dot_general x7, matrix products, attend(): jnp.einsum('hqk,hkd->hqd', weights.astype(jnp.bfloat16), value_pair, pref...  30.3 us
  transfers between devices with their start and end apart: 3, of which 2 were waited for; matrix products, arithmetic and copies ran while one was open for 7% of the time, Pallas kernels for 0%

profile of v1, /device:TPU:0, one launch (start us, length us, event | category | flops | bytes accessed | tf_op | source)
XLA Modules:
  0.0 1065.2 jit_solution(18047029676874547460)
XLA Ops:
  12.2 9.7 multiply_select_fusion.1
  21.9 9.2 copy.489
  31.0 38.0 %reshape.2370 = f32[8,32,16,32,16]{4,3,2,1,0:T(8,128)} reshape(f32[8,512,512]{2,1,0:T(8,128)} %copy.489) | data formatting | bytes 16777216 | tf_op jit(solution)/shard_map/vmap()/reshape | solution.py:13
  69.0 21.5 %select_reduce_fusion = f32[8,32,16,16]{3,2,1,0:T(8,128)S(1)} fusion(f32[8,32,16,32,16]{4,3,2,1,0:T(8,128)} %reshape.2370, pred[32,32]{1,0:T(8,128)(4,1)S(1)} %iota_compare_fusion.9), kind=kLoop, calls=%fused_computation.26 | loop fusion | flops 4128768 | bytes 8651776 | tf_op jit(solution)/shard_map/vmap()/reduce_sum | solution.py:15
  92.5 5.5 fusion.121
  99.1 5.9 fusion.120
  105.5 6.1 fusion.119
  112.2 5.9 fusion.118
  118.7 6.3 fusion.117
  124.9 6.0 fusion.116
  131.5 20.9 %reshape.2371 = f32[8,16,32,16,32]{2,1,4,3,0:T(8,128)} reshape(f32[8,512,512]{1,2,0:T(8,128)} %multiply_select_fusion.1) | data formatting | bytes 16777216 | tf_op jit(solution)/shard_map/vmap()/reshape | solution.py:13
  153.0 12.9 %reshape.2373 = f32[8,8,64,8,64]{2,1,4,3,0:T(8,128)} reshape(f32[8,512,512]{1,2,0:T(8,128)} %multiply_select_fusion.1) | data formatting | bytes 16777216 | tf_op jit(solution)/shard_map/vmap()/reshape | solution.py:13
  166.5 9.9 reshape.2375
  176.9 10.9 %reshape.2377 = f32[8,2,256,2,256]{2,1,4,3,0:T(2,128)} reshape(f32[8,512,512]{1,2,0:T(8,128)} %multiply_select_fusion.1) | data formatting | bytes 16777216 | tf_op jit(solution)/shard_map/vmap()/reshape | solution.py:13
  476.0 3.5 fusion.97
  479.8 3.6 fusion.96
  483.4 4.2 constant_dynamic-update-slice_fusion.1
  487.8 4.0 constant_dynamic-update-slice_fusion
  491.9 4.8 subtract_dynamic-update-slice_fusion
  497.4 13.7 %select_reduce_fusion.1 = f32[8,16,32,32]{2,1,3,0:T(8,128)S(1)} fusion(f32[8,16,32,16,32]{2,1,4,3,0:T(8,128)} %reshape.2371, pred[16,16]{0,1:T(8,128)(4,1)S(1)} %copy-done.76), kind=kLoop, calls=%fused_computation.27 | loop fusion | flops 4063232 | bytes 8913152 | tf_op jit(solution)/shard_map/vmap()/reduce_sum | solution.py:15
  517.9 9.5 select_reduce_fusion.2
  533.0 6.7 select_reduce_fusion.4
  544.0 12.8 %select_reduce_fusion.3 = f32[8,2,256,256]{2,1,3,0:T(2,128)} fusion(f32[8,2,256,2,256]{2,1,4,3,0:T(2,128)} %reshape.2377, pred[2,2]{0,1:T(4,128)(4,1)S(1)} %copy-done.79), kind=kLoop, calls=%fused_computation.44 | loop fusion | flops 3145728 | bytes 12582916 | tf_op jit(solution)/shard_map/vmap()/reduce_sum | solution.py:15
  565.7 5.1 fusion.54
  570.9 3.4 negate_bitcast_fusion
  577.5 6.1 broadcast_select_fusion
  583.6 26.1 %fusion.22 = f32[8,512,640]{2,1,0:T(8,128)} fusion(f32[8,512,128]{1,2,0:T(8,128)S(1)} %copy-done.1, f32[8,512,512]{1,2,0:T(8,128)} %broadcast_select_fusion, f32[8,1,256,256]{3,2,0,1:T(8,128)} %get-tuple-element.267, f32[8,1,256,256]{3,2,0,1:T(8,128)} %get-tuple-element.266, f32[8,1,256,256]{3,2,0,1:T(8,128)} %negate_bitcast_fusion), kind=kOutput, calls=%fused_computation.29 | convolution fusion | flops 16117137408 | bytes 27262976 | tf_op jit(solution)/shard_map/vmap()/dot_general | solution.py:60
  616.1 4.4 fusion.74
  625.2 15.6 %subtract_convert_fusion = bf16[8,512,128]{2,1,0:T(8,128)(2,1)S(1)} fusion(f32[8,512,128]{1,2,0:T(8,128)S(1)} %copy-done.1, f32[8,512,640]{2,1,0:T(8,128)} %fusion.22, bf16[512,8,128]{2,0,1:T(8,128)(2,1)S(1)} %copy.751, f32[8,512]{1,0:T(8,128)S(1)} %copy-done.11), kind=kOutput, calls=%fused_computation.82 | convolution fusion | flops 3223322624 | bytes 12599296 | tf_op jit(solution)/shard_map/vmap()/dot_general | solution.py:76
  647.2 4.9 fusion.88
  655.4 16.7 %convert_subtract_fusion = f32[8,512,128]{2,1,0:T(8,128)} fusion(f32[8,512,512]{2,1,0:T(8,128)S(1)} %fusion.88, f32[8,512]{1,0:T(8,128)S(1)} %copy-done.11, pred[512,512]{0,1:T(8,128)(4,1)S(1)} %iota_compare_fusion.7, bf16[512,8,128]{2,0,1:T(8,128)(2,1)S(1)} %copy-done.3, f32[8,512,640]{2,1,0:T(8,128)} %fusion.22), kind=kOutput, calls=%fused_computation.88 | convolution fusion | flops 3226468352 | bytes 13910016 | tf_op jit(solution)/shard_map/vmap()/dot_general | solution.py:85
  674.1 28.3 %all-gather.1 = bf16[8,1,512]{2,1,0:T(2,128)(2,1)S(1)} all-gather(bf16[1,1,512]{2,1,0:T(2,128)(2,1)S(1)} %reshape.2388), channel_id=1, replica_groups=mesh['ctx'=8,'head'=4] {'ctx'}, dimensions={0}, use_global_device_ids=true | all-gather | bytes 9216 | tf_op jit(solution)/shard_map/all_gather | solution.py:164
  702.7 19.2 %fusion.35 = f32[8,512,512]{1,2,0:T(8,128)S(1)} fusion(f32[8,512,640]{2,1,0:T(8,128)} %fusion.22, f32[8,512,512]{2,1,0:T(8,128)} %copy-done.2, f32[8,512]{1,0:T(8,128)S(1)} %copy-done.11, pred[512,512]{0,1:T(8,128)(4,1)S(1)} %iota_compare_fusion.7), kind=kOutput, calls=%fused_computation.49 | convolution fusion | flops 12889096192 | bytes 25444352 | tf_op jit(solution)/shard_map/vmap()/dot_general | solution.py:82
  728.1 4.2 convert.2
  732.2 168.9 %all-gather.5.cloned.1.call-done = bf16[16,4096,128]{2,1,0:T(8,128)(2,1)} async-done(((bf16[16,512,128]{2,1,0:T(8,128)(2,1)}), bf16[16,4096,128]{2,1,0:T(8,128)(2,1)}) %all-gather.5.cloned.1.call-update) | async-done | bytes 16777232 | tf_op jit(solution)/shard_map/all_gather | solution.py:156
  901.2 11.4 %fusion.114 = (bf16[8,4096,128]{2,1,0:T(8,128)(2,1)}, bf16[8,4096,128]{2,1,0:T(8,128)(2,1)}) fusion(bf16[16,4096,128]{2,1,0:T(8,128)(2,1)} %all-gather.5.cloned.1.call-done), kind=kLoop, calls=%fused_computation.193 | loop fusion | bytes 33554432 | tf_op jit(solution)/shard_map/split | solution.py:155
  912.6 91.0 %while.19 = (s32[]{:T(128)}, f32[8,512,128]{1,2,0:T(8,128)S(1)}, f32[8,512]{1,0:T(8,128)S(1)}, f32[8,512]{1,0:T(8,128)S(1)}, f32[8,512,128]{2,1,0:T(8,128)}, /*i...) while((s32[]{:T(128)}, f32[8,512,128]{1,2,0:T(8,128)S(1)}, ...), condition=%wide.region_11.12_spmd, body=%wide.region_8.11_spmd.sunk | while | flops 1904222208 | bytes 60563748 | solution.py:177
  918.0 4.3 multiply_add_fusion.5
  922.3 3.4 convolution_bitcast_fusion.2
  931.0 4.3 multiply_add_fusion.5
  935.3 3.4 convolution_bitcast_fusion.2
  943.9 4.3 multiply_add_fusion.5
  956.9 4.3 multiply_add_fusion.5
  969.9 4.3 multiply_add_fusion.5
  982.8 4.3 multiply_add_fusion.5
  995.8 4.3 multiply_add_fusion.5
  1005.8 9.5 convolution_convert_fusion
  1015.4 42.8 %reduce-scatter.2.cloned.1.call-done = bf16[128,4096]{1,0:T(8,128)(2,1)} async-done(((bf16[512,4096]{1,0:T(8,128)(2,1)}), bf16[128,4096]{1,0:T(8,128)(2,1)}) %reduce-scatter.2.cloned.1.call-update) | async-done | bytes 1048592 | tf_op jit(solution)/shard_map/reduce_scatter | solution.py:180
  (570 shorter events, 413.4 us)
Async XLA Ops:
  6.5 721.5 %all-gather.7.cloned.1.call-start = ((), (), s32[]{:S(2)}) async-start(), calls=%async_computation.3 | async-start | bytes 2359296 | tf_op jit(solution)/shard_map/all_gather | solution.py:161
  7.2 182.2 %copy-start.42 = (f32[16]{0:T(128)}, f32[16]{0:T(128)S(1)}, u32[]{:S(2)}) copy-start(f32[16]{0:T(128)S(1)} %get-tuple-element.401) | copy-start | bytes 196
  454.8 18.2 %copy-start.13 = (f32[8,16,2]{1,2,0:T(2,128)S(1)}, f32[8,16,2]{1,2,0:T(2,128)}, u32[]{:S(2)}) copy-start(f32[8,16,2]{1,2,0:T(2,128)} %copy.591) | copy-start | bytes 3076
  454.8 18.2 %copy-start.14 = (f32[8,16,2]{1,2,0:T(2,128)S(1)}, f32[8,16,2]{1,2,0:T(2,128)}, u32[]{:S(2)}) copy-start(f32[8,16,2]{1,2,0:T(2,128)} %copy.593) | copy-start | bytes 3076
  454.8 18.2 %copy-start.15 = (f32[8,16,2]{1,2,0:T(2,128)S(1)}, f32[8,16,2]{1,2,0:T(2,128)}, u32[]{:S(2)}) copy-start(f32[8,16,2]{1,2,0:T(2,128)} %copy.595) | copy-start | bytes 3076
  454.8 18.2 %copy-start.16 = (f32[8,16,2]{1,2,0:T(2,128)S(1)}, f32[8,16,2]{1,2,0:T(2,128)}, u32[]{:S(2)}) copy-start(f32[8,16,2]{1,2,0:T(2,128)} %copy.597) | copy-start | bytes 3076
  454.9 18.3 %copy-start.17 = (f32[8,16,2]{1,2,0:T(2,128)S(1)}, f32[8,16,2]{1,2,0:T(2,128)}, u32[]{:S(2)}) copy-start(f32[8,16,2]{1,2,0:T(2,128)} %copy.599) | copy-start | bytes 3076
  454.9 21.0 %copy-start.18 = (f32[8,16,2]{1,2,0:T(2,128)S(1)}, f32[8,16,2]{1,2,0:T(2,128)}, u32[]{:S(2)}) copy-start(f32[8,16,2]{1,2,0:T(2,128)} %copy.601) | copy-start | bytes 3076
  454.9 21.0 %copy-start.19 = (f32[8,16,2]{1,2,0:T(2,128)S(1)}, f32[8,16,2]{1,2,0:T(2,128)}, u32[]{:S(2)}) copy-start(f32[8,16,2]{1,2,0:T(2,128)} %copy.603) | copy-start | bytes 3076
  454.9 21.0 %copy-start.20 = (f32[8,16,2]{1,2,0:T(2,128)S(1)}, f32[8,16,2]{1,2,0:T(2,128)}, u32[]{:S(2)}) copy-start(f32[8,16,2]{1,2,0:T(2,128)} %copy.605) | copy-start | bytes 3076
  454.9 21.0 %copy-start.21 = (f32[8,16,2]{1,2,0:T(2,128)S(1)}, f32[8,16,2]{1,2,0:T(2,128)}, u32[]{:S(2)}) copy-start(f32[8,16,2]{1,2,0:T(2,128)} %copy.607) | copy-start | bytes 3076
  454.9 21.0 %copy-start.22 = (f32[8,16,2]{1,2,0:T(2,128)S(1)}, f32[8,16,2]{1,2,0:T(2,128)}, u32[]{:S(2)}) copy-start(f32[8,16,2]{1,2,0:T(2,128)} %copy.609) | copy-start | bytes 3076
  454.9 21.0 %copy-start.23 = (f32[8,16,2]{1,2,0:T(2,128)S(1)}, f32[8,16,2]{1,2,0:T(2,128)}, u32[]{:S(2)}) copy-start(f32[8,16,2]{1,2,0:T(2,128)} %copy.611) | copy-start | bytes 3076
  454.9 21.0 %copy-start.24 = (f32[8,16,2]{1,2,0:T(2,128)S(1)}, f32[8,16,2]{1,2,0:T(2,128)}, u32[]{:S(2)}) copy-start(f32[8,16,2]{1,2,0:T(2,128)} %copy.613) | copy-start | bytes 3076
  454.9 21.0 %copy-start.25 = (f32[8,16,2]{1,2,0:T(2,128)S(1)}, f32[8,16,2]{1,2,0:T(2,128)}, u32[]{:S(2)}) copy-start(f32[8,16,2]{1,2,0:T(2,128)} %copy.615) | copy-start | bytes 3076
  454.9 21.0 %copy-start.26 = (f32[8,16,2]{1,2,0:T(2,128)S(1)}, f32[8,16,2]{1,2,0:T(2,128)}, u32[]{:S(2)}) copy-start(f32[8,16,2]{1,2,0:T(2,128)} %copy.617) | copy-start | bytes 3076
  455.0 21.0 %copy-start.27 = (f32[8,16,2]{1,2,0:T(2,128)S(1)}, f32[8,16,2]{1,2,0:T(2,128)}, u32[]{:S(2)}) copy-start(f32[8,16,2]{1,2,0:T(2,128)} %copy.619) | copy-start | bytes 3076
  455.0 21.0 %copy-start.28 = (f32[8,16,2]{1,2,0:T(2,128)S(1)}, f32[8,16,2]{1,2,0:T(2,128)}, u32[]{:S(2)}) copy-start(f32[8,16,2]{1,2,0:T(2,128)} %copy.621) | copy-start | bytes 3076
  459.4 20.1 %copy-start.30 = (f32[8,16,2]{1,2,0:T(2,128)S(1)}, f32[8,16,2]{1,2,0:T(2,128)}, u32[]{:S(2)}) copy-start(f32[8,16,2]{1,2,0:T(2,128)} %copy.623) | copy-start | bytes 3076
  459.4 20.1 %copy-start.31 = (f32[8,16,2]{1,2,0:T(2,128)S(1)}, f32[8,16,2]{1,2,0:T(2,128)}, u32[]{:S(2)}) copy-start(f32[8,16,2]{1,2,0:T(2,128)} %copy.625) | copy-start | bytes 3076
  459.4 20.2 %copy-start.32 = (f32[8,16,2]{1,2,0:T(2,128)S(1)}, f32[8,16,2]{1,2,0:T(2,128)}, u32[]{:S(2)}) copy-start(f32[8,16,2]{1,2,0:T(2,128)} %copy.627) | copy-start | bytes 3076
  459.4 20.2 %copy-start.33 = (f32[8,16,2]{1,2,0:T(2,128)S(1)}, f32[8,16,2]{1,2,0:T(2,128)}, u32[]{:S(2)}) copy-start(f32[8,16,2]{1,2,0:T(2,128)} %copy.629) | copy-start | bytes 3076
  459.4 20.2 %copy-start.34 = (f32[8,16,2]{1,2,0:T(2,128)S(1)}, f32[8,16,2]{1,2,0:T(2,128)}, u32[]{:S(2)}) copy-start(f32[8,16,2]{1,2,0:T(2,128)} %copy.631) | copy-start | bytes 3076
  459.5 20.2 %copy-start.35 = (f32[8,16,2]{1,2,0:T(2,128)S(1)}, f32[8,16,2]{1,2,0:T(2,128)}, u32[]{:S(2)}) copy-start(f32[8,16,2]{1,2,0:T(2,128)} %copy.633) | copy-start | bytes 3076
  459.5 20.2 %copy-start.36 = (f32[8,16,2]{1,2,0:T(2,128)S(1)}, f32[8,16,2]{1,2,0:T(2,128)}, u32[]{:S(2)}) copy-start(f32[8,16,2]{1,2,0:T(2,128)} %copy.635) | copy-start | bytes 3076
  459.5 20.2 %copy-start.37 = (f32[8,16,2]{1,2,0:T(2,128)S(1)}, f32[8,16,2]{1,2,0:T(2,128)}, u32[]{:S(2)}) copy-start(f32[8,16,2]{1,2,0:T(2,128)} %copy.637) | copy-start | bytes 3076
  459.5 20.2 %copy-start.38 = (f32[8,16,2]{1,2,0:T(2,128)S(1)}, f32[8,16,2]{1,2,0:T(2,128)}, u32[]{:S(2)}) copy-start(f32[8,16,2]{1,2,0:T(2,128)} %copy.639) | copy-start | bytes 3076
  459.5 20.2 %copy-start.39 = (f32[8,16,2]{1,2,0:T(2,128)S(1)}, f32[8,16,2]{1,2,0:T(2,128)}, u32[]{:S(2)}) copy-start(f32[8,16,2]{1,2,0:T(2,128)} %copy.641) | copy-start | bytes 3076
  459.5 20.2 %copy-start.40 = (f32[8,16,2]{1,2,0:T(2,128)S(1)}, f32[8,16,2]{1,2,0:T(2,128)}, u32[]{:S(2)}) copy-start(f32[8,16,2]{1,2,0:T(2,128)} %copy.643) | copy-start | bytes 3076
  459.5 20.2 %copy-start.41 = (f32[8,16,2]{1,2,0:T(2,128)S(1)}, f32[8,16,2]{1,2,0:T(2,128)}, u32[]{:S(2)}) copy-start(f32[8,16,2]{1,2,0:T(2,128)} %copy.645) | copy-start | bytes 3076
  466.7 20.9 %copy-start.47 = (f32[8,16,2]{1,2,0:T(2,128)S(1)}, f32[8,16,2]{1,2,0:T(2,128)}, u32[]{:S(2)}) copy-start(f32[8,16,2]{1,2,0:T(2,128)} %copy.673) | copy-start | bytes 3076
  466.7 20.9 %copy-start.48 = (f32[8,16,2]{1,2,0:T(2,128)S(1)}, f32[8,16,2]{1,2,0:T(2,128)}, u32[]{:S(2)}) copy-start(f32[8,16,2]{1,2,0:T(2,128)} %copy.675) | copy-start | bytes 3076
  466.7 20.9 %copy-start.49 = (f32[8,16,2]{1,2,0:T(2,128)S(1)}, f32[8,16,2]{1,2,0:T(2,128)}, u32[]{:S(2)}) copy-start(f32[8,16,2]{1,2,0:T(2,128)} %copy.677) | copy-start | bytes 3076
  466.7 20.9 %copy-start.50 = (f32[8,16,2]{1,2,0:T(2,128)S(1)}, f32[8,16,2]{1,2,0:T(2,128)}, u32[]{:S(2)}) copy-start(f32[8,16,2]{1,2,0:T(2,128)} %copy.679) | copy-start | bytes 3076
  466.7 20.9 %copy-start.51 = (f32[8,16,2]{1,2,0:T(2,128)S(1)}, f32[8,16,2]{1,2,0:T(2,128)}, u32[]{:S(2)}) copy-start(f32[8,16,2]{1,2,0:T(2,128)} %copy.681) | copy-start | bytes 3076
  466.7 20.9 %copy-start.52 = (f32[8,16,2]{1,2,0:T(2,128)S(1)}, f32[8,16,2]{1,2,0:T(2,128)}, u32[]{:S(2)}) copy-start(f32[8,16,2]{1,2,0:T(2,128)} %copy.683) | copy-start | bytes 3076
  466.7 20.9 %copy-start.53 = (f32[8,16,2]{1,2,0:T(2,128)S(1)}, f32[8,16,2]{1,2,0:T(2,128)}, u32[]{:S(2)}) copy-start(f32[8,16,2]{1,2,0:T(2,128)} %copy.685) | copy-start | bytes 3076
  466.7 20.9 %copy-start.54 = (f32[8,16,2]{1,2,0:T(2,128)S(1)}, f32[8,16,2]{1,2,0:T(2,128)}, u32[]{:S(2)}) copy-start(f32[8,16,2]{1,2,0:T(2,128)} %copy.687) | copy-start | bytes 3076
  470.6 17.0 %copy-start.55 = (f32[8,16,2]{1,2,0:T(2,128)S(1)}, f32[8,16,2]{1,2,0:T(2,128)}, u32[]{:S(2)}) copy-start(f32[8,16,2]{1,2,0:T(2,128)} %copy.689) | copy-start | bytes 3076
  470.6 17.0 %copy-start.56 = (f32[8,16,2]{1,2,0:T(2,128)S(1)}, f32[8,16,2]{1,2,0:T(2,128)}, u32[]{:S(2)}) copy-start(f32[8,16,2]{1,2,0:T(2,128)} %copy.691) | copy-start | bytes 3076
  470.6 17.0 %copy-start.57 = (f32[8,16,2]{1,2,0:T(2,128)S(1)}, f32[8,16,2]{1,2,0:T(2,128)}, u32[]{:S(2)}) copy-start(f32[8,16,2]{1,2,0:T(2,128)} %copy.693) | copy-start | bytes 3076
  470.7 17.0 %copy-start.58 = (f32[8,16,2]{1,2,0:T(2,128)S(1)}, f32[8,16,2]{1,2,0:T(2,128)}, u32[]{:S(2)}) copy-start(f32[8,16,2]{1,2,0:T(2,128)} %copy.695) | copy-start | bytes 3076
  479.7 12.1 %copy-start.64 = (f32[16]{0:T(128)S(1)}, f32[16]{0:T(128)}, u32[]{:S(2)}) copy-start(f32[16]{0:T(128)} %get-tuple-element.406) | copy-start | bytes 196
  479.7 12.1 %copy-start.65 = (f32[8,16,2]{1,2,0:T(2,128)S(1)}, f32[8,16,2]{1,2,0:T(2,128)}, u32[]{:S(2)}) copy-start(f32[8,16,2]{1,2,0:T(2,128)} %copy.701) | copy-start | bytes 3076
  620.6 280.6 %all-gather.5.cloned.1.call-start = ((), (), s32[]{:S(2)}) async-start(), calls=%async_computation.1 | async-start | bytes 18874368 | tf_op jit(solution)/shard_map/all_gather | solution.py:156
  625.2 15.7 %copy-start.5 = (bf16[512,8,128]{2,0,1:T(8,128)(2,1)S(1)}, bf16[512,8,128]{2,0,1:T(8,128)(2,1)}, u32[]{:S(2)}) copy-start(bf16[512,8,128]{2,0,1:T(8,128)(2,1)} %copy.760) | copy-start | bytes 3145732
  642.4 415.8 %reduce-scatter.2.cloned.1.call-start = ((), (), s32[]{:S(2)}) async-start(), calls=%async_computation.2 | async-start | bytes 5242880 | tf_op jit(solution)/shard_map/reduce_scatter | solution.py:180
  702.7 19.2 %copy-start.4 = (bf16[512,8,128]{2,0,1:T(8,128)(2,1)S(1)}, bf16[512,8,128]{2,0,1:T(8,128)(2,1)}, u32[]{:S(2)}) copy-start(bf16[512,8,128]{2,0,1:T(8,128)(2,1)} %copy.483) | copy-start | bytes 3145732
  (48 other events, 297.1 us)
Sparse Core Ops, SparseCore 0:
  620.7 51.9 all-gather.6
  674.9 226.2 all-gather.4
  1015.5 42.6 reduce-scatter.1
